TPU v7x, 128 devices: a whole 4x4x4 slice. The times are simulated.
128 devices in a mesh: chaos: 8 (over x, y_hi), space: 16 (over y_lo, z, core).
Axes of the slice: x: 4, y: 4 (y_hi: 2, y_lo: 2; y = y_hi * 2 + y_lo), z: 4, core: 2. Of those that a mesh axis runs over, the one named last changes fastest.
Arguments:
- modes: float32 [120, 128, 2048], P('chaos', 'space'), may hold values from -2 to 2
- kl_fields: float32 [8, 128, 2048], P(None, 'space'), may hold values from 0.1 to 1
- triples: int32 [624, 3], replicated, may hold values from 0 to 119, as said below
- ratios: int32 [624, 2], replicated, may hold values from 1 to 12, as said below
- mode_of_slot: int32 [120], replicated, may hold values from 0 to 119, each once
Outputs:
- applied: float32 [120, 128, 2048], P('chaos', 'space')
Inputs may be any that keep to these rules, and one draw needn't show every extreme that they name: `triples`: rows are distinct. Modes are the multi-indices of total degree at most 3 in 7 variables. Every mode i has the row (i, i, 0); every other row (i, j, k) has k of 1 or more, and the multi-indices of i and j differ by one in variable k and agree elsewhere; each such pair appears in both orders. `ratios`: column 0 is a positive numerator, column 1 a denominator of 1 to 4. `mode_of_slot`: A permutation.
All inputs are finite; a program needn't handle non-finite values.
Results may differ from a plain program's by a relative error of at most 0.000082.
Values sent between devices are 32-bit elements; how exact they have to be, the bound alone decides.
No kernel may reach another device: no remote copies, remote signals or barrier semaphores. Data moves between devices by JAX's collectives and lax.ppermute only.
A program may use at most 128 MiB of HBM per device.

v0:
```python
import jax
import jax.numpy as jnp
from jax import lax
from jax.sharding import PartitionSpec as P

HIGHEST_PRECISION = lax.Precision.HIGHEST


def extended_2(x, sides, width):
    for axis, dim in sides:
        count, length = (lax.axis_size(axis), x.shape[dim])
        up = [(i, (i + 1) % count) for i in range(count - 1)]
        down = [(j, i) for i, j in up]
        last = lax.slice_in_dim(x, length - width, length, axis=dim)
        first = lax.slice_in_dim(x, 0, width, axis=dim)
        before = lax.ppermute(last, axis, up)
        after = lax.ppermute(first, axis, down)
        x = jnp.concatenate([before, x, after], axis=dim)
    return x


def from_root(block, axis, owner):
    block = jnp.where(lax.axis_index(axis) == owner, block, jnp.zeros_like(block))
    return lax.psum(block, axis)


def diffuse(values, factor):
    center = values[:, 1:-1, :]
    coef_mid = factor[1:-1, :]
    result = (coef_mid + factor[:-2, :]) * (center - values[:, :-2, :])
    result = result + (coef_mid + factor[2:, :]) * (center - values[:, 2:, :])
    zero_col = jnp.zeros_like(center[:, :, :1])
    left_cell = jnp.concatenate([zero_col, center[:, :, :-1]], axis=2)
    right_cell = jnp.concatenate([center[:, :, 1:], zero_col], axis=2)
    coef_zero = jnp.zeros_like(coef_mid[:, :1])
    coef_left = jnp.concatenate([coef_zero, coef_mid[:, :-1]], axis=1)
    coef_right = jnp.concatenate([coef_mid[:, 1:], coef_zero], axis=1)
    result = result + (coef_mid + coef_left) * (center - left_cell)
    result = result + (coef_mid + coef_right) * (center - right_cell)
    return 0.5 * result


def coupling_table(triples, ratios, mode_of_slot, kl_terms, mode_count):
    matches = triples[:, :2, None] == mode_of_slot[None, None, :]
    slot_pairs = jnp.sum(jnp.where(matches, jnp.arange(mode_count, dtype=jnp.int32), 0), axis=2)
    weights = ratios[:, 0].astype(jnp.float32) / ratios[:, 1].astype(jnp.float32)
    flat_index = (triples[:, 2] * mode_count + slot_pairs[:, 0]) * mode_count + slot_pairs[:, 1]
    coupling = (
        jnp.zeros((kl_terms * mode_count * mode_count,), jnp.float32).at[flat_index].add(weights)
    )
    return coupling.reshape(kl_terms, mode_count, mode_count)


def local(modes, kl_fields, triples, ratios, mode_of_slot):
    groups = lax.axis_size("chaos")
    own_modes = modes.shape[0]
    mode_count = own_modes * groups
    kl_terms = kl_fields.shape[0]
    slab_rows = modes.shape[1]
    raster_cols = modes.shape[2]
    first_slot = lax.axis_index("chaos") * own_modes
    coupling = coupling_table(triples, ratios, mode_of_slot, kl_terms, mode_count)
    local_rows = lax.dynamic_slice_in_dim(coupling, first_slot, own_modes, 1).reshape(
        kl_terms * own_modes, mode_count
    )
    joined = jnp.concatenate([modes, kl_fields], axis=0)
    padded = extended_2(joined, (("space", 1),), 1)
    source = padded[:own_modes]
    coefficients = padded[own_modes:]
    rim_depth = source.shape[1]
    flat_source = source.reshape(own_modes, rim_depth * raster_cols)
    zero_sum = jnp.zeros((kl_terms * own_modes, rim_depth * raster_cols), jnp.float32)
    mixed_fields = zero_sum
    for owner in range(groups):
        received = from_root(flat_source, "chaos", owner)
        mode_block = lax.dynamic_slice_in_dim(local_rows, owner * own_modes, received.shape[0], 1)
        mixed_fields = mixed_fields + jnp.dot(
            mode_block, received, precision=HIGHEST_PRECISION, preferred_element_type=jnp.float32
        )
    extended = mixed_fields.reshape(kl_terms, own_modes, rim_depth, raster_cols)
    applied = jnp.zeros((own_modes, slab_rows, raster_cols), jnp.float32)
    for kl_index in range(kl_terms):
        applied = applied + diffuse(extended[kl_index], coefficients[kl_index])
    return applied


def solution(mesh):
    return jax.shard_map(
        local,
        mesh=mesh,
        in_specs=(P("chaos", "space", None), P(None, "space", None), P(), P(), P()),
        out_specs=P("chaos", "space", None),
        check_vma=False,
    )
```

profile of v0, /device:TPU:5, one launch (start us, length us, event | category | flops | bytes accessed | tf_op | source)
XLA Modules:
  0.0 603.4 jit_solution(7292626513668426113)
XLA Ops:
  8.2 2.6 collective-permute-start.1
  10.9 3.4 collective-permute-start
  18.4 1.8 copy.47
  20.5 1.8 copy.40
  22.5 1.9 copy.41
  24.7 1.8 copy.42
  27.8 1.8 copy.46
  29.8 1.9 copy.43
  31.9 1.8 copy.44
  34.0 1.9 copy.45
  36.8 4.9 scatter_custom_fusion
  46.8 419.7 %all-reduce.35.cloned.1.call-done = (f32[15,20480]{1,0:T(8,128)}, f32[15,20480]{1,0:T(8,128)}, f32[15,20480]{1,0:T(8,128)}, f32[15,20480]{1,0:T(8,128)}, f32[15,...) async-done(((f32[15,20480]{1,0:T(8,128)}, f32[15,20480]{1,0:T(8,128)}, f32[15,20480]{1,0:T(8,128)}, f32[15,20480]{1,0:T(8,128)}, ...) | async-done | bytes 9830416 | tf_op jit(solution)/shard_map/psum | solution.py:24
  466.5 9.2 %fusion.75 = f32[120,20480]{1,0:T(8,128)S(1)} fusion(f32[15,20480]{1,0:T(8,128)} %get-tuple-element.5, f32[120,120]{1,0:T(8,128)S(1)} %reshape.94), kind=kOutput, calls=%fused_computation.142 | convolution fusion | flops 442368000 | bytes 11116800 | tf_op jit(solution)/shard_map/dot_general | solution.py:77
  475.8 8.2 %convolution_add_fusion.6 = f32[120,20480]{1,0:T(8,128)S(1)} fusion(f32[120,20480]{1,0:T(8,128)S(1)} %fusion.75, f32[15,20480]{1,0:T(8,128)S(1)} %copy-done.13, f32[120,120]{1,0:T(8,128)S(1)} %reshape.94), kind=kOutput, calls=%fused_computation.7 | convolution fusion | flops 444825600 | bytes 20947200 | tf_op jit(solution)/shard_map/dot_general | solution.py:77
  484.0 8.3 %convolution_add_fusion.5 = f32[120,20480]{1,0:T(8,128)S(1)} fusion(f32[120,20480]{1,0:T(8,128)S(1)} %convolution_add_fusion.6, f32[15,20480]{1,0:T(8,128)S(1)} %copy-done.12, f32[120,120]{1,0:T(8,128)S(1)} %reshape.94), kind=kOutput, calls=%fused_computation.6 | convolution fusion | flops 444825600 | bytes 20947200 | tf_op jit(solution)/shard_map/dot_general | solution.py:77
  492.3 7.9 %convolution_add_fusion.4 = f32[120,20480]{1,0:T(8,128)S(1)} fusion(f32[120,20480]{1,0:T(8,128)S(1)} %convolution_add_fusion.5, f32[15,20480]{1,0:T(8,128)S(1)} %copy-done.11, f32[120,120]{1,0:T(8,128)S(1)} %reshape.94), kind=kOutput, calls=%fused_computation.5 | convolution fusion | flops 444825600 | bytes 20947200 | tf_op jit(solution)/shard_map/dot_general | solution.py:77
  500.3 8.1 %convolution_add_fusion.3 = f32[120,20480]{1,0:T(8,128)S(1)} fusion(f32[120,20480]{1,0:T(8,128)S(1)} %convolution_add_fusion.4, f32[15,20480]{1,0:T(8,128)S(1)} %copy-done.10, f32[120,120]{1,0:T(8,128)S(1)} %reshape.94), kind=kOutput, calls=%fused_computation.4 | convolution fusion | flops 444825600 | bytes 20947200 | tf_op jit(solution)/shard_map/dot_general | solution.py:77
  508.4 7.9 %convolution_add_fusion.2 = f32[120,20480]{1,0:T(8,128)S(1)} fusion(f32[120,20480]{1,0:T(8,128)S(1)} %convolution_add_fusion.3, f32[15,20480]{1,0:T(8,128)S(1)} %copy-done.9, f32[120,120]{1,0:T(8,128)S(1)} %reshape.94), kind=kOutput, calls=%fused_computation.3 | convolution fusion | flops 444825600 | bytes 20947200 | tf_op jit(solution)/shard_map/dot_general | solution.py:77
  516.4 10.0 %convolution_add_fusion.1 = f32[120,20480]{1,0:T(8,128)S(1)} fusion(f32[120,20480]{1,0:T(8,128)S(1)} %convolution_add_fusion.2, f32[15,20480]{1,0:T(8,128)S(1)} %copy-done.8, f32[120,120]{1,0:T(8,128)S(1)} %reshape.94), kind=kOutput, calls=%fused_computation.2 | convolution fusion | flops 444825600 | bytes 20947200 | tf_op jit(solution)/shard_map/dot_general | solution.py:77
  526.4 10.8 %convolution_add_fusion = f32[120,20480]{1,0:T(8,128)} fusion(f32[120,20480]{1,0:T(8,128)S(1)} %convolution_add_fusion.1, f32[15,20480]{1,0:T(8,128)S(1)} %copy-done.7, f32[120,120]{1,0:T(8,128)S(1)} %reshape.94), kind=kOutput, calls=%fused_computation.1 | convolution fusion | flops 444825600 | bytes 20947200 | tf_op jit(solution)/shard_map/dot_general | solution.py:77
  537.1 8.7 %fusion.80 = (f32[15,20480]{1,0:T(8,128)}, f32[15,20480]{1,0:T(8,128)}, f32[15,20480]{1,0:T(8,128)}, f32[15,20480]{1,0:T(8,128)}, f32[15,20480]{1,0:T(8,128)}, /...) fusion(f32[120,20480]{1,0:T(8,128)} %convolution_add_fusion), kind=kLoop, calls=%fused_computation.162 | loop fusion | bytes 19660800 | tf_op jit(solution)/shard_map/slice | solution.py:83
  547.6 3.1 squeeze.44
  550.7 3.1 squeeze.43
  553.8 3.0 squeeze.42
  556.8 3.1 squeeze.20
  559.9 3.1 squeeze.19
  563.0 3.0 squeeze.18
  567.8 4.2 fusion.81
  572.0 2.6 fusion.83
  575.4 2.6 fusion.85
  579.0 2.6 fusion.87
  581.7 14.4 %fusion.5 = f32[15,8,2048]{2,1,0:T(8,128)} fusion(f32[15,10,2048]{2,1,0:T(8,128)S(1)} %copy-done, f32[15,10,2048]{2,1,0:T(8,128)S(1)} %copy-done.1, f32[15,10,2048]{2,1,0:T(8,128)S(1)} %copy-done.2, f32[15,10,2048]{2,1,0:T(8,128)S(1)} %copy-done.3, f32[15,10,2048]{2,1,0:T(8,128)} %squeeze.19, f32[15,10,2048]{2,1,0:T(8,128)} %squeeze.18, ...), kind=kLoop, calls=%fused_computation.16 | loop fusion | flops 23592960 | bytes 42394112 | tf_op jit(solution)/shard_map/add | solution.py:83
  (104 shorter events, 19.7 us)
Async XLA Ops:
  6.5 1.3 copy-start.6
  6.5 460.0 %all-reduce.35.cloned.1.call-start = ((), (), s32[]{:S(2)}) async-start(), calls=%async_computation | async-start | bytes 20971520 | tf_op jit(solution)/shard_map/psum | solution.py:24
  8.2 7.5 %collective-permute-start.1 = (f32[23,1,2048]{2,0,1:T(8,128)S(1)}, f32[23,1,2048]{2,0,1:T(8,128)S(1)}, u32[]{:S(2)}, u32[]{:S(2)}) collective-permute-start(f32[23,1,2048]{2,0,1:T(8,128)S(1)} %copy.36), channel_id=1, source_target_pairs={{1,0},{2,1},{3,2},{4,3},{5,4},{6,5},{7,6},{8,7},{9,8},{10,9},{11,1... | collective-permute-start | bytes 565256 | tf_op jit(solution)/shard_map/ppermute | solution.py:17
  10.9 6.0 %collective-permute-start = (f32[23,1,2048]{2,0,1:T(8,128)S(1)}, f32[23,1,2048]{2,0,1:T(8,128)S(1)}, u32[]{:S(2)}, u32[]{:S(2)}) collective-permute-start(f32[23,1,2048]{2,0,1:T(8,128)S(1)} %copy.34), channel_id=1, source_target_pairs={{0,1},{1,2},{2,3},{3,4},{4,5},{5,6},{6,7},{7,8},{8,9},{9,10},{10,1... | collective-permute-start | bytes 565256 | tf_op jit(solution)/shard_map/ppermute | solution.py:16
  466.5 9.3 %copy-start.13 = (f32[15,20480]{1,0:T(8,128)S(1)}, f32[15,20480]{1,0:T(8,128)}, u32[]{:S(2)}) copy-start(f32[15,20480]{1,0:T(8,128)} %get-tuple-element.6) | copy-start | bytes 3686404
  475.8 8.2 %copy-start.12 = (f32[15,20480]{1,0:T(8,128)S(1)}, f32[15,20480]{1,0:T(8,128)}, u32[]{:S(2)}) copy-start(f32[15,20480]{1,0:T(8,128)} %get-tuple-element.7) | copy-start | bytes 3686404
  483.9 8.4 %copy-start.11 = (f32[15,20480]{1,0:T(8,128)S(1)}, f32[15,20480]{1,0:T(8,128)}, u32[]{:S(2)}) copy-start(f32[15,20480]{1,0:T(8,128)} %get-tuple-element.8) | copy-start | bytes 3686404
  492.3 7.9 %copy-start.10 = (f32[15,20480]{1,0:T(8,128)S(1)}, f32[15,20480]{1,0:T(8,128)}, u32[]{:S(2)}) copy-start(f32[15,20480]{1,0:T(8,128)} %get-tuple-element.9) | copy-start | bytes 3686404
  500.3 8.1 %copy-start.9 = (f32[15,20480]{1,0:T(8,128)S(1)}, f32[15,20480]{1,0:T(8,128)}, u32[]{:S(2)}) copy-start(f32[15,20480]{1,0:T(8,128)} %get-tuple-element.10) | copy-start | bytes 3686404
  508.4 7.9 %copy-start.8 = (f32[15,20480]{1,0:T(8,128)S(1)}, f32[15,20480]{1,0:T(8,128)}, u32[]{:S(2)}) copy-start(f32[15,20480]{1,0:T(8,128)} %get-tuple-element.11) | copy-start | bytes 3686404
  516.4 10.0 %copy-start.7 = (f32[15,20480]{1,0:T(8,128)S(1)}, f32[15,20480]{1,0:T(8,128)}, u32[]{:S(2)}) copy-start(f32[15,20480]{1,0:T(8,128)} %get-tuple-element.12) | copy-start | bytes 3686404
  567.8 4.2 copy-start.4
  567.8 4.2 copy-start.5
  572.0 2.6 copy-start.2
  572.0 3.5 copy-start.3
  575.4 2.6 copy-start
  575.4 3.5 copy-start.1
  578.9 2.7 copy-start.14
  578.9 2.7 copy-start.15
  578.9 2.7 copy-start.16
  578.9 2.7 copy-start.17
  578.9 2.7 copy-start.18
  578.9 2.7 copy-start.19
  578.9 2.7 copy-start.20
  579.0 2.7 copy-start.21
  579.0 2.7 copy-start.22
  579.0 2.7 copy-start.23
  579.0 2.7 copy-start.24
  579.0 2.7 copy-start.25
  579.0 2.7 copy-start.26
  579.0 2.7 copy-start.27
  579.0 2.7 copy-start.28
  (4 other events, 3.1 us)
Sparse Core Ops, SparseCore 0:
  36.0 430.4 all-reduce.34
where the time goes:
time: 612 us; the launch traced here: 603 us
  waiting for transfers between devices  422 us (69%)
  matrix products  70.4 us (12%)
  local copies, waits for them, and re-layouts  64.6 us (11%)
  other arithmetic  25.7 us (4%)
  between operations  14.4 us (2%)
    psum x1, waiting for transfers between devices, from_root(): return lax.psum(block, axis)  420 us
    dot_general x8, matrix products, local(): jnp.dot(mode_block, received, precision=HIGHEST_PRECISION, preferred_elem...  70.4 us
    squeeze x8, local copies, waits for them, and re-layouts, local(): applied = applied + diffuse(extended[kl_index], coefficients[kl_index])  21.9 us
    unnamed x81, local copies, waits for them, and re-layouts  19.7 us
    add x1, other arithmetic, local(): applied = applied + diffuse(extended[kl_index], coefficients[kl_index])  14.4 us
  transfers between devices with their start and end apart: 3, of which 3 were waited for; matrix products, arithmetic and copies ran while one was open for 2% of the time, Pallas kernels for 0%

commit v1 on v0

--- a/solution.py
+++ b/solution.py
@@ -2,6 +2,7 @@
 import jax.numpy as jnp
 from jax import lax
 from jax.sharding import PartitionSpec as P
+from jax.lax import all_gather
 
 HIGHEST_PRECISION = lax.Precision.HIGHEST
 
@@ -21,7 +22,10 @@
 
 def from_root(block, axis, owner):
     block = jnp.where(lax.axis_index(axis) == owner, block, jnp.zeros_like(block))
-    return lax.psum(block, axis)
+    finish_the_samples_all = lambda field_in, mesh_name: all_gather(
+        field_in, axis_name=mesh_name
+    ).sum(axis=0)
+    return finish_the_samples_all(block, axis)
 
 
 def diffuse(values, factor):

time: 612 us -> 1140 us (1.86)
  waiting for transfers between devices: 422 us -> 891 us
  other arithmetic: 25.7 us -> 74.6 us
    all_gather x0 -> x8, waiting for transfers between devices: none -> 888 us  [from_root(): all_gather(field_in, axis_name=mesh_name).sum(axis=0)]
    psum x1 -> x0, waiting for transfers between devices: 420 us -> none  [from_root(): return lax.psum(block, axis)]
    reduce_sum x0 -> x8, other arithmetic: none -> 43.4 us  [from_root(): finish_the_samples_all = lambda field_in, mesh_name: all_gather(field_in,...]
    select_n x0 -> x8, local copies, waits for them, and re-layouts: none -> 25.4 us  [from_root(): jnp.where(lax.axis_index(axis) == owner, block, jnp.zeros_like(block))]
    unnamed x81 -> x59, local copies, waits for them, and re-layouts: 19.7 us -> 3.19 us
  transfers between devices with their start and end apart: 3 -> 10, of which waited for: 3 -> 10; matrix products, arithmetic and copies ran while one was open for 2% -> 12% of each run, Pallas kernels for 0% -> 0%
where the time goes in v1:
time: 1140 us; the launch traced here: 1130 us
  waiting for transfers between devices  891 us (78%)
  other arithmetic  74.6 us (7%)
  matrix products  73.2 us (6%)
  local copies, waits for them, and re-layouts  72.9 us (6%)
  between operations  14.5 us (1%)
    all_gather x8, waiting for transfers between devices, from_root(): all_gather(field_in, axis_name=mesh_name).sum(axis=0)  888 us
    dot_general x8, matrix products, local(): jnp.dot(mode_block, received, precision=HIGHEST_PRECISION, preferred_elem...  73.2 us
    reduce_sum x8, other arithmetic, from_root(): finish_the_samples_all = lambda field_in, mesh_name: all_gather(field_in,...  43.4 us
    select_n x8, local copies, waits for them, and re-layouts, from_root(): jnp.where(lax.axis_index(axis) == owner, block, jnp.zeros_like(block))  25.4 us
  transfers between devices with their start and end apart: 10, of which 10 were waited for; matrix products, arithmetic and copies ran while one was open for 12% of the time, Pallas kernels for 0%

profile of v1, /device:TPU:5, one launch (start us, length us, event | category | flops | bytes accessed | tf_op | source)
XLA Modules:
  0.0 1132.6 jit_solution(17266581427809191896)
XLA Ops:
  10.9 3.4 collective-permute-start
  17.1 3.7 broadcast_select_fusion
  30.5 3.7 broadcast_select_fusion.1
  40.7 3.4 select_n.158
  50.9 4.9 scatter_custom_fusion
  60.9 93.4 %all-gather.9.cloned.1.call-done = f32[8,15,20480]{2,1,0:T(8,128)} async-done(((f32[1,15,20480]{2,1,0:T(8,128)}), f32[8,15,20480]{2,1,0:T(8,128)}) %all-gather.9.cloned.1.call-update) | async-done | bytes 9830416 | tf_op jit(solution)/shard_map/all_gather | solution.py:25
  154.3 5.9 reduce_sum.82
  160.2 122.0 %all-gather.11.cloned.1.call-done = f32[8,15,20480]{2,1,0:T(8,128)} async-done(((f32[1,15,20480]{2,1,0:T(8,128)}), f32[8,15,20480]{2,1,0:T(8,128)}) %all-gather.11.cloned.1.call-update) | async-done | bytes 9830416 | tf_op jit(solution)/shard_map/all_gather | solution.py:25
  282.1 4.8 reduce_sum.83
  286.9 123.1 %all-gather.13.cloned.1.call-done = f32[8,15,20480]{2,1,0:T(8,128)} async-done(((f32[1,15,20480]{2,1,0:T(8,128)}), f32[8,15,20480]{2,1,0:T(8,128)}) %all-gather.13.cloned.1.call-update) | async-done | bytes 9830416 | tf_op jit(solution)/shard_map/all_gather | solution.py:25
  410.0 5.8 reduce_sum.84
  415.9 121.9 %all-gather.21.cloned.1.call-done = f32[8,15,20480]{2,1,0:T(8,128)} async-done(((f32[1,15,20480]{2,1,0:T(8,128)}), f32[8,15,20480]{2,1,0:T(8,128)}) %all-gather.21.cloned.1.call-update) | async-done | bytes 9830416 | tf_op jit(solution)/shard_map/all_gather | solution.py:25
  537.7 4.8 reduce_sum.88
  542.5 122.9 %all-gather.15.cloned.1.call-done = f32[8,15,20480]{2,1,0:T(8,128)} async-done(((f32[1,15,20480]{2,1,0:T(8,128)}), f32[8,15,20480]{2,1,0:T(8,128)}) %all-gather.15.cloned.1.call-update) | async-done | bytes 9830416 | tf_op jit(solution)/shard_map/all_gather | solution.py:25
  665.4 5.8 reduce_sum.85
  671.2 121.9 %all-gather.17.cloned.1.call-done = f32[8,15,20480]{2,1,0:T(8,128)} async-done(((f32[1,15,20480]{2,1,0:T(8,128)}), f32[8,15,20480]{2,1,0:T(8,128)}) %all-gather.17.cloned.1.call-update) | async-done | bytes 9830416 | tf_op jit(solution)/shard_map/all_gather | solution.py:25
  793.1 5.8 reduce_sum.86
  798.9 122.0 %all-gather.19.cloned.1.call-done = f32[8,15,20480]{2,1,0:T(8,128)} async-done(((f32[1,15,20480]{2,1,0:T(8,128)}), f32[8,15,20480]{2,1,0:T(8,128)}) %all-gather.19.cloned.1.call-update) | async-done | bytes 9830416 | tf_op jit(solution)/shard_map/all_gather | solution.py:25
  921.0 5.8 reduce_sum.87
  926.8 9.4 fusion.75
  936.2 7.9 convolution_add_fusion.6
  944.1 8.4 convolution_add_fusion.5
  952.5 8.1 convolution_add_fusion.4
  960.6 7.9 convolution_add_fusion.3
  968.6 8.2 convolution_add_fusion.2
  976.7 10.8 convolution_add_fusion.1
  987.6 61.3 %all-gather.23.cloned.1.call-done = f32[8,15,20480]{2,1,0:T(8,128)} async-done(((f32[1,15,20480]{2,1,0:T(8,128)}), f32[8,15,20480]{2,1,0:T(8,128)}) %all-gather.23.cloned.1.call-update) | async-done | bytes 9830416 | tf_op jit(solution)/shard_map/all_gather | solution.py:25
  1048.8 4.8 reduce_sum.89
  1053.6 12.6 %convolution_add_fusion = f32[120,20480]{1,0:T(8,128)} fusion(f32[120,20480]{1,0:T(8,128)} %convolution_add_fusion.1, f32[15,20480]{1,0:T(8,128)S(1)} %reduce_sum.89, f32[120,120]{1,0:T(8,128)S(1)} %reshape.174), kind=kOutput, calls=%fused_computation.1 | convolution fusion | flops 444825600 | bytes 20947200 | tf_op jit(solution)/shard_map/dot_general | solution.py:81
  1066.2 8.8 fusion.80
  1096.9 4.2 fusion.81
  1110.8 14.5 %fusion.5 = f32[15,8,2048]{2,1,0:T(8,128)} fusion(f32[15,10,2048]{2,1,0:T(8,128)S(1)} %copy-done, f32[15,10,2048]{2,1,0:T(8,128)S(1)} %copy-done.1, f32[15,10,2048]{2,1,0:T(8,128)S(1)} %copy-done.2, f32[15,10,2048]{2,1,0:T(8,128)S(1)} %copy-done.3, f32[15,10,2048]{2,1,0:T(8,128)} %squeeze.19, f32[15,10,2048]{2,1,0:T(8,128)} %squeeze.18, ...), kind=kLoop, calls=%fused_computation.16 | loop fusion | flops 23592960 | bytes 42394112 | tf_op jit(solution)/shard_map/add | solution.py:87
  (119 shorter events, 66.4 us)
Async XLA Ops:
  6.5 147.8 %all-gather.9.cloned.1.call-start = ((), (), s32[]{:S(2)}) async-start(), calls=%async_computation | async-start | bytes 11796480 | tf_op jit(solution)/shard_map/all_gather | solution.py:25
  8.2 7.5 collective-permute-start.1
  10.9 6.0 collective-permute-start
  24.0 258.1 %all-gather.11.cloned.1.call-start = ((), (), s32[]{:S(2)}) async-start(), calls=%async_computation.1 | async-start | bytes 11796480 | tf_op jit(solution)/shard_map/all_gather | solution.py:25
  27.2 382.8 %all-gather.13.cloned.1.call-start = ((), (), s32[]{:S(2)}) async-start(), calls=%async_computation.2 | async-start | bytes 11796480 | tf_op jit(solution)/shard_map/all_gather | solution.py:25
  30.4 507.3 %all-gather.21.cloned.1.call-start = ((), (), s32[]{:S(2)}) async-start(), calls=%async_computation.6 | async-start | bytes 11796480 | tf_op jit(solution)/shard_map/all_gather | solution.py:25
  37.3 628.1 %all-gather.15.cloned.1.call-start = ((), (), s32[]{:S(2)}) async-start(), calls=%async_computation.3 | async-start | bytes 11796480 | tf_op jit(solution)/shard_map/all_gather | solution.py:25
  40.7 752.4 %all-gather.17.cloned.1.call-start = ((), (), s32[]{:S(2)}) async-start(), calls=%async_computation.4 | async-start | bytes 11796480 | tf_op jit(solution)/shard_map/all_gather | solution.py:25
  44.2 876.8 %all-gather.19.cloned.1.call-start = ((), (), s32[]{:S(2)}) async-start(), calls=%async_computation.5 | async-start | bytes 11796480 | tf_op jit(solution)/shard_map/all_gather | solution.py:25
  47.4 1001.5 %all-gather.23.cloned.1.call-start = ((), (), s32[]{:S(2)}) async-start(), calls=%async_computation.7 | async-start | bytes 11796480 | tf_op jit(solution)/shard_map/all_gather | solution.py:25
  47.4 3.2 slice-start
  47.4 3.2 copy-start.28
  47.4 3.3 copy-start.26
  47.5 3.4 copy-start.27
  936.2 7.9 copy-start.7
  944.1 8.4 copy-start.8
  952.5 8.1 copy-start.9
  960.6 7.9 copy-start.10
  1096.9 4.2 copy-start.4
  1096.9 4.2 copy-start.5
  1101.1 3.5 copy-start.3
  1104.5 3.5 copy-start.1
  1108.0 2.7 copy-start.15
  1108.0 2.7 copy-start.16
  1108.0 2.7 copy-start.17
  1108.0 2.7 copy-start.18
  1108.1 2.7 copy-start.19
  1108.1 2.7 copy-start.20
  1108.1 2.7 copy-start.21
  1108.1 2.7 copy-start.22
  1108.1 2.7 copy-start.23
  1108.1 2.7 copy-start.24
  (8 other events, 19.9 us)
Sparse Core Ops, SparseCore 0:
  24.2 130.0 all-gather.8
  156.6 125.4 all-gather.10
  284.5 125.4 all-gather.12
  412.2 125.4 all-gather.20
  539.9 125.4 all-gather.14
  667.6 125.4 all-gather.16
  795.4 125.4 all-gather.18
  923.3 125.5 all-gather.22
